TPU v7x, 256 devices: a whole 4x4x8 slice. The times are simulated.
256 devices in a mesh: person: 2 (over x_lo), tm: 32 (over y, z), mp: 4 (over x_hi, core).
Axes of the slice: x: 4 (x_hi: 2, x_lo: 2; x = x_hi * 2 + x_lo), y: 4, z: 8, core: 2. Of those that a mesh axis runs over, the one named last changes fastest.
Arguments:
- motion: bfloat16 [2, 2, 8192, 2048], P('person', None, 'tm', 'mp'), may hold values from -6 to 6
- valid: int32 [2, 2, 8192], P('person', None, 'tm'), may hold values from 0 to 1, as said below
- windows: int32 [32], replicated, may hold values from 64 to 512, as said below
- gains: float32 [2, 2048], replicated, may hold values from 0.5 to 1.5
- w_self_in: bfloat16 [2048, 3072], P('tm', 'mp')
- w_self_out: bfloat16 [2048, 2048], P('mp', 'tm'), may hold values from -0.125 to 0.125
- w_cross_in: bfloat16 [2048, 3072], P('tm', 'mp')
- w_cross_out: bfloat16 [2048, 2048], P('mp', 'tm'), may hold values from -0.125 to 0.125
Outputs:
- mixed: bfloat16 [2, 2, 8192, 2048], P('person', None, 'tm', 'mp')
Inputs may be any that keep to these rules, and one draw needn't show every extreme that they name: `valid`: for each person and clip the frames with 1 form a prefix that covers at least half of the 8192 frames and never all of them. `windows`: some head's window is exactly 512.
All inputs are finite; a program needn't handle non-finite values.
Results may differ from a plain program's by a relative error of at most 0.035.
The roundings to bfloat16 on the way count: a program that leaves them out, or rounds other values in their place, can miss the bound.
Values may be sent and summed in bfloat16 or wider, within the bound.
No kernel may reach another device: no remote copies, remote signals or barrier semaphores. Data moves between devices by JAX's collectives and lax.ppermute only.
A program may use at most 64 MiB of HBM per device.

v0:
```python
import jax
import jax.numpy as jnp
from jax import lax
from jax.sharding import PartitionSpec as P

D = 2048
HEADS = 32
KV_HEADS = 8
HEAD_DIM = 64
WIN = 512


EPS = 1e-05


def passed_along(value, axis, steps):
    count = lax.axis_size(axis)
    leading, last = (max(0, -steps), min(count, count - steps))
    return lax.ppermute(value, axis, [(source, source + steps) for source in range(leading, last)])


def swapped(value, axis, apart):
    mask = 2**apart
    pairs = [(source, source ^ mask) for source in range(lax.axis_size(axis))]
    return lax.ppermute(value, axis, pairs)


def rms_normed(rows, gain):
    values = rows.astype(jnp.float32)
    scale = lax.rsqrt(jnp.mean(values * values, axis=-1, keepdims=True) + EPS)
    return (values * scale * gain).astype(jnp.bfloat16)


def project_in(normed_rows, weight_rows):
    total = jnp.dot(
        normed_rows,
        lax.all_gather(weight_rows, "tm", axis=0, tiled=True),
        preferred_element_type=jnp.float32,
    )
    return total.astype(jnp.bfloat16)


def earlier_frames(pair, frames):
    pieces = [pair]
    for step in range(1, WIN // frames + 1):
        pieces.insert(0, passed_along((pair[0], pair[1]), "tm", step))
    key_vals = jnp.concatenate([piece[0] for piece in pieces], 1)
    masks = jnp.concatenate([piece[1] for piece in pieces], 1)
    return (key_vals, masks)


def window_attend(queries, key_vals, masks, wins):
    count_q = queries.shape[1]
    count_k = key_vals.shape[1]
    dist = jnp.arange(count_q)[:, None] + (count_k - count_q) - jnp.arange(count_k)[None, :]

    def one_clip(items):
        query, pairs, kvalid = items
        keys = pairs[:, :, 0]
        values = pairs[:, :, 1]
        allowed = (
            (dist >= 0)
            & (dist < wins[:, :, None, None])
            & ((kvalid[None, None, None, :] == 1) | (dist == 0))
        )
        scores = jnp.einsum(
            "qkgd,ckd->kgqc", query, keys, preferred_element_type=jnp.float32
        ) * HEAD_DIM ** (-0.5)
        top = jnp.max(jnp.where(allowed, scores, -1e30), axis=-1, keepdims=True)
        exps = jnp.where(allowed, jnp.exp(scores - top), 0.0)
        total = jnp.sum(exps, axis=-1)
        weights = exps.astype(jnp.bfloat16)
        summed = jnp.einsum("kgqc,ckd->qkgd", weights, values, preferred_element_type=jnp.float32)
        return (summed / jnp.transpose(total, (2, 0, 1))[..., None]).astype(jnp.bfloat16)

    outputs = lax.map(one_clip, (queries, key_vals, masks))
    return outputs.reshape(outputs.shape[0] * outputs.shape[1], -1)


def project_out(heads, weight, residual):
    terms = jnp.dot(
        heads, lax.all_gather(weight, "tm", axis=1, tiled=True), preferred_element_type=jnp.float32
    )
    summed = lax.psum_scatter(terms, "mp", scatter_dimension=1, tiled=True)
    return (residual.astype(jnp.float32) + summed).astype(jnp.bfloat16)


def body(motion, valid, windows, gains, w_self_in, w_self_out, w_cross_in, w_cross_out):
    clips = motion.shape[1]
    frames = motion.shape[2]
    count = clips * frames
    group = HEADS // KV_HEADS
    local_heads = w_self_out.shape[0] // HEAD_DIM
    local_groups = local_heads // group
    wins = lax.dynamic_slice_in_dim(
        windows, lax.axis_index("mp") * local_heads, local_heads, 0
    ).reshape(local_groups, group)
    own_valid = valid[0]
    residual = motion.reshape(count, motion.shape[3])
    full = lax.all_gather(motion, "mp", axis=3, tiled=True).reshape(count, D)
    normed = rms_normed(full, gains[0])
    self_proj = project_in(normed, w_self_in).reshape(
        clips, frames, local_groups, group + 2, HEAD_DIM
    )
    self_pair = self_proj[:, :, :, group:]
    key_vals, masks = earlier_frames((self_pair, own_valid), frames)
    self_heads = window_attend(self_proj[:, :, :, :group], key_vals, masks, wins)
    hidden = project_out(self_heads, w_self_out, residual)
    hidden_full = lax.all_gather(hidden, "mp", axis=1, tiled=True)
    normed2 = rms_normed(hidden_full, gains[1])
    cross_proj = project_in(normed2, w_cross_in).reshape(
        clips, frames, local_groups, group + 2, HEAD_DIM
    )
    cross_pair = cross_proj[:, :, :, group:]
    partner = swapped((cross_pair, own_valid), "person", 0)
    partner_vals, partner_masks = earlier_frames(partner, frames)
    cross_heads = window_attend(cross_proj[:, :, :, :group], partner_vals, partner_masks, wins)
    mixed = project_out(cross_heads, w_cross_out, hidden)
    return mixed.reshape(motion.shape)


def solution(mesh):
    in_specs = (
        P("person", None, "tm", "mp"),
        P("person", None, "tm"),
        P(),
        P(),
        P("tm", "mp"),
        P("mp", "tm"),
        P("tm", "mp"),
        P("mp", "tm"),
    )
    out_specs = P("person", None, "tm", "mp")
    return jax.shard_map(body, mesh=mesh, in_specs=in_specs, out_specs=out_specs, check_vma=False)
```

profile of v0, /device:TPU:1, one launch (start us, length us, event | category | flops | bytes accessed | tf_op | source)
XLA Modules:
  0.0 520.7 jit_solution(5809093448599657538)
XLA Ops:
  9.6 32.9 %all-gather.7.cloned.1.call-done = bf16[1,2,256,2048]{3,2,1,0:T(8,128)(2,1)} async-done(((bf16[1,2,256,512]{3,2,1,0:T(8,128)(2,1)}), bf16[1,2,256,2048]{3,2,1,0:T(8,128)(2,1)}) %all-gather.7.cloned.1.call-update) | async-done | bytes 2097168 | tf_op jit(solution)/shard_map/all_gather | solution.py:100
  45.3 74.5 %all-gather.9.cloned.1.call-done = bf16[2048,768]{1,0:T(8,128)(2,1)} async-done(((bf16[64,768]{1,0:T(8,128)(2,1)}), bf16[2048,768]{1,0:T(8,128)(2,1)}) %all-gather.9.cloned.1.call-update) | async-done | bytes 3145744 | tf_op jit(solution)/shard_map/all_gather | solution.py:37
  119.8 3.7 convolution_convert_fusion
  124.1 3.5 collective-permute-start
  127.6 3.1 collective-permute-start.1
  130.8 3.1 collective-permute-start.2
  133.9 2.4 collective-permute-start.3
  136.4 5.5 %collective-permute-done.2 = s32[2,256]{1,0:T(2,128)S(1)} collective-permute-done((s32[2,256]{1,0:T(2,128)S(1)}, s32[2,256]{1,0:T(2,128)S(1)}, u32[]{:S(2)}, u32[]{:S(2)}) %collective-permute-start.2) | collective-permute-done | bytes 2080 | tf_op jit(solution)/shard_map/ppermute | solution.py:19
  143.4 19.0 %while.24 = (s32[]{:T(128)}, bf16[2,256,2,4,64]{1,4,3,2,0:T(8,128)(2,1)S(1)}, bf16[2,768,2,2,64]{1,4,2,3,0:T(8,128)(2,1)S(1)}, s32[8]{0:T(128)S(1)}, s32[2,768]{...) while((s32[]{:T(128)}, ...), condition=%wide.region_4.5_spmd.clone.clone, body=%wide.region_1.4_spmd.clone.clone.sunk | while | flops 625673728 | bytes 12019361 | solution.py:76
  143.9 6.4 %fusion.149 = (f32[2,4,256]{2,1,0:T(4,128)S(1)}, bf16[2,4,256,768]{2,3,1,0:T(8,128)(2,1)}) fusion(s32[2,4]{1,0:T(2,128)S(1)} %lt.125, s32[256,768]{0,1:T(8,128)S(1)} %iota_subtract_fusion.4, pred[256,768]{0,1:T(8,128)(4,1)S(1)} %get-tuple-element.308, pred[256,768]{0,1:T(8,128)(4,1)S(1)} %get-tuple-element.309, ...), kind=kOutput, calls=%fused_computation.100.clone.1 | convolution fusion | flops 423101184 | bytes 6433792 | tf_op jit(solution)/shard_map/while/body/eval_jaxpr/sub | solution.py:70
  150.3 2.5 fusion.150
  153.4 6.4 %fusion.149 = (f32[2,4,256]{2,1,0:T(4,128)S(1)}, bf16[2,4,256,768]{2,3,1,0:T(8,128)(2,1)}) fusion(s32[2,4]{1,0:T(2,128)S(1)} %lt.125, s32[256,768]{0,1:T(8,128)S(1)} %iota_subtract_fusion.4, pred[256,768]{0,1:T(8,128)(4,1)S(1)} %get-tuple-element.308, pred[256,768]{0,1:T(8,128)(4,1)S(1)} %get-tuple-element.309, ...), kind=kOutput, calls=%fused_computation.100.clone.1 | convolution fusion | flops 423101184 | bytes 6433792 | tf_op jit(solution)/shard_map/while/body/eval_jaxpr/sub | solution.py:70
  159.8 2.5 fusion.150
  163.0 33.2 %all-gather.11.cloned.1.call-done = bf16[512,2048]{0,1:T(8,128)(2,1)} async-done(((bf16[512,64]{0,1:T(8,128)(2,1)}), bf16[512,2048]{0,1:T(8,128)(2,1)}) %all-gather.11.cloned.1.call-update) | async-done | bytes 2097168 | tf_op jit(solution)/shard_map/all_gather | solution.py:82
  196.2 4.9 fusion.122
  201.2 58.2 %reduce-scatter.3.cloned.1.call-done = f32[512,512]{1,0:T(8,128)} async-done(((f32[512,2048]{1,0:T(8,128)}), f32[512,512]{1,0:T(8,128)}) %reduce-scatter.3.cloned.1.call-update) | async-done | bytes 1048592 | tf_op jit(solution)/shard_map/reduce_scatter | solution.py:84
  262.4 28.5 %all-gather.13.cloned.1.call-done = bf16[512,2048]{1,0:T(8,128)(2,1)} async-done(((bf16[512,512]{1,0:T(8,128)(2,1)}), bf16[512,2048]{1,0:T(8,128)(2,1)}) %all-gather.13.cloned.1.call-update) | async-done | bytes 2097168 | tf_op jit(solution)/shard_map/all_gather | solution.py:109
  293.0 75.1 %all-gather.15.cloned.1.call-done = bf16[2048,768]{1,0:T(8,128)(2,1)} async-done(((bf16[64,768]{1,0:T(8,128)(2,1)}), bf16[2048,768]{1,0:T(8,128)(2,1)}) %all-gather.15.cloned.1.call-update) | async-done | bytes 3145744 | tf_op jit(solution)/shard_map/all_gather | solution.py:37
  368.1 4.4 fusion.107
  374.5 4.0 collective-permute-done.4
  378.4 3.4 collective-permute-start.5
  381.9 3.2 collective-permute-start.6
  387.6 3.1 collective-permute-start.8
  390.6 2.4 collective-permute-start.9
  396.9 19.0 %while.25 = (s32[]{:T(128)}, bf16[2,256,2,4,64]{1,4,3,2,0:T(8,128)(2,1)S(1)}, bf16[2,768,2,2,64]{1,4,2,3,0:T(8,128)(2,1)S(1)}, s32[8]{0:T(128)S(1)}, s32[2,768]{...) while((s32[]{:T(128)}, ...), condition=%wide.region_10.11_spmd.clone.clone, body=%wide.region_7.10_spmd.clone.clone.sunk | while | flops 625673728 | bytes 12019361 | solution.py:76
  397.4 6.4 %fusion.155 = (f32[2,4,256]{2,1,0:T(4,128)S(1)}, bf16[2,4,256,768]{2,3,1,0:T(8,128)(2,1)}) fusion(s32[2,4]{1,0:T(2,128)S(1)} %lt.129, s32[256,768]{0,1:T(8,128)S(1)} %iota_subtract_fusion.5, pred[256,768]{0,1:T(8,128)(4,1)S(1)} %get-tuple-element.319, pred[256,768]{0,1:T(8,128)(4,1)S(1)} %get-tuple-element.320, ...), kind=kOutput, calls=%fused_computation.101.clone.1 | convolution fusion | flops 423101184 | bytes 6433792 | tf_op jit(solution)/shard_map/while/body/eval_jaxpr/sub | solution.py:70
  403.8 2.6 fusion.156
  406.9 6.4 %fusion.155 = (f32[2,4,256]{2,1,0:T(4,128)S(1)}, bf16[2,4,256,768]{2,3,1,0:T(8,128)(2,1)}) fusion(s32[2,4]{1,0:T(2,128)S(1)} %lt.129, s32[256,768]{0,1:T(8,128)S(1)} %iota_subtract_fusion.5, pred[256,768]{0,1:T(8,128)(4,1)S(1)} %get-tuple-element.319, pred[256,768]{0,1:T(8,128)(4,1)S(1)} %get-tuple-element.320, ...), kind=kOutput, calls=%fused_computation.101.clone.1 | convolution fusion | flops 423101184 | bytes 6433792 | tf_op jit(solution)/shard_map/while/body/eval_jaxpr/sub | solution.py:70
  413.3 2.5 fusion.156
  416.5 31.9 %all-gather.17.cloned.1.call-done = bf16[512,2048]{0,1:T(8,128)(2,1)} async-done(((bf16[512,64]{0,1:T(8,128)(2,1)}), bf16[512,2048]{0,1:T(8,128)(2,1)}) %all-gather.17.cloned.1.call-update) | async-done | bytes 2097168 | tf_op jit(solution)/shard_map/all_gather | solution.py:82
  448.4 4.9 fusion.123
  453.4 58.3 %reduce-scatter.5.cloned.1.call-done = f32[512,512]{1,0:T(8,128)} async-done(((f32[512,2048]{1,0:T(8,128)}), f32[512,512]{1,0:T(8,128)}) %reduce-scatter.5.cloned.1.call-update) | async-done | bytes 1048592 | tf_op jit(solution)/shard_map/reduce_scatter | solution.py:84
  (89 shorter events, 26.6 us)
Async XLA Ops:
  6.5 36.0 %all-gather.7.cloned.1.call-start = ((), (), s32[]{:S(2)}) async-start(), calls=%async_computation.2 | async-start | bytes 2621440 | tf_op jit(solution)/shard_map/all_gather | solution.py:100
  7.3 112.5 %all-gather.9.cloned.1.call-start = ((), (), s32[]{:S(2)}) async-start(), calls=%async_computation.3 | async-start | bytes 3244032 | tf_op jit(solution)/shard_map/all_gather | solution.py:37
  8.0 188.2 %all-gather.11.cloned.1.call-start = ((), (), s32[]{:S(2)}) async-start(), calls=%async_computation.4 | async-start | bytes 2162688 | tf_op jit(solution)/shard_map/all_gather | solution.py:82
  8.7 250.7 %reduce-scatter.3.cloned.1.call-start = ((), (), s32[]{:S(2)}) async-start(), calls=%async_computation.5 | async-start | bytes 5242880 | tf_op jit(solution)/shard_map/reduce_scatter | solution.py:84
  42.5 2.2 copy-start
  123.5 7.3 %copy-start.3 = (s32[1,2,256]{2,1,0:T(2,128)S(1)}, s32[1,2,256]{2,1,0:T(2,128)}, u32[]{:S(2)}) copy-start(s32[1,2,256]{2,1,0:T(2,128)} %param.13) | copy-start | bytes 6148
  123.5 12.9 %copy-start.4 = (s32[32]{0:T(128)S(1)}, s32[32]{0:T(128)}, u32[]{:S(2)}) copy-start(s32[32]{0:T(128)} %param.14) | copy-start | bytes 388
  124.1 18.3 %collective-permute-start = (bf16[2,256,2,2,64]{1,0,4,3,2:T(2,128)(2,1)S(1)}, bf16[2,256,2,2,64]{1,0,4,3,2:T(2,128)(2,1)S(1)}, u32[]{:S(2)}, u32[]{:S(2)}) collective-permute-start(bf16[2,256,2,2,64]{1,0,4,3,2:T(2,128)(2,1)S(1)} %slice.48), channel_id=1, source_target_pairs={{0,8},{4,12},{8,16},{12,20},{16,24},{20,28},{24,32},{28,36},{32,40... | collective-permute-start | bytes 786440 | tf_op jit(solution)/shard_map/ppermute | solution.py:19
  127.6 14.8 %collective-permute-start.1 = (bf16[2,256,2,2,64]{1,0,4,3,2:T(2,128)(2,1)S(1)}, bf16[2,256,2,2,64]{1,0,4,3,2:T(2,128)(2,1)S(1)}, u32[]{:S(2)}, u32[]{:S(2)}) collective-permute-start(bf16[2,256,2,2,64]{1,0,4,3,2:T(2,128)(2,1)S(1)} %slice.48), channel_id=1, source_target_pairs={{0,4},{4,8},{8,12},{12,16},{16,20},{20,24},{24,28},{28,32},{32,36}... | collective-permute-start | bytes 786440 | tf_op jit(solution)/shard_map/ppermute | solution.py:19
  130.8 11.1 %collective-permute-start.2 = (s32[2,256]{1,0:T(2,128)S(1)}, s32[2,256]{1,0:T(2,128)S(1)}, u32[]{:S(2)}, u32[]{:S(2)}) collective-permute-start(s32[2,256]{1,0:T(2,128)S(1)} %bitcast.216), channel_id=1, source_target_pairs={{0,8},{4,12},{8,16},{12,20},{16,24},{20,28},{24,32},{28,36},{32,40... | collective-permute-start | bytes 6152 | tf_op jit(solution)/shard_map/ppermute | solution.py:19
  133.9 8.1 %collective-permute-start.3 = (s32[2,256]{1,0:T(2,128)S(1)}, s32[2,256]{1,0:T(2,128)S(1)}, u32[]{:S(2)}, u32[]{:S(2)}) collective-permute-start(s32[2,256]{1,0:T(2,128)S(1)} %bitcast.217), channel_id=1, source_target_pairs={{0,4},{4,8},{8,12},{12,16},{16,20},{20,24},{24,28},{28,32},{32,36}... | collective-permute-start | bytes 6152 | tf_op jit(solution)/shard_map/ppermute | solution.py:19
  201.2 58.3 %copy-start.2 = (bf16[1,2,256,512]{3,2,1,0:T(8,128)(2,1)S(1)}, bf16[1,2,256,512]{3,2,1,0:T(8,128)(2,1)}, u32[]{:S(2)}) copy-start(bf16[1,2,256,512]{3,2,1,0:T(8,128)(2,1)} %param.12) | copy-start | bytes 1572868
  201.2 89.8 %all-gather.13.cloned.1.call-start = ((), (), s32[]{:S(2)}) async-start(), calls=%async_computation.6 | async-start | bytes 2621440 | tf_op jit(solution)/shard_map/all_gather | solution.py:109
  261.6 106.5 %all-gather.15.cloned.1.call-start = ((), (), s32[]{:S(2)}) async-start(), calls=%async_computation.7 | async-start | bytes 3244032 | tf_op jit(solution)/shard_map/all_gather | solution.py:37
  262.2 186.2 %all-gather.17.cloned.1.call-start = ((), (), s32[]{:S(2)}) async-start(), calls=%async_computation.8 | async-start | bytes 2162688 | tf_op jit(solution)/shard_map/all_gather | solution.py:82
  373.1 5.3 %collective-permute-start.4 = (bf16[2,256,2,2,64]{1,0,4,3,2:T(2,128)(2,1)S(1)}, bf16[2,256,2,2,64]{1,0,4,3,2:T(2,128)(2,1)S(1)}, u32[]{:S(2)}, u32[]{:S(2)}) collective-permute-start(bf16[2,256,2,2,64]{1,0,4,3,2:T(2,128)(2,1)S(1)} %slice.50), channel_id=1, source_target_pairs={{0,128},{128,0},{1,129},{129,1},{2,130},{130,2},{3,131},{131,3},{4... | collective-permute-start | bytes 786440 | tf_op jit(solution)/shard_map/ppermute | solution.py:25
  374.4 137.2 %reduce-scatter.5.cloned.1.call-start = ((), (), s32[]{:S(2)}) async-start(), calls=%async_computation.9 | async-start | bytes 5242880 | tf_op jit(solution)/shard_map/reduce_scatter | solution.py:84
  378.4 17.5 %collective-permute-start.5 = (bf16[2,256,2,2,64]{1,0,4,3,2:T(2,128)(2,1)S(1)}, bf16[2,256,2,2,64]{1,0,4,3,2:T(2,128)(2,1)S(1)}, u32[]{:S(2)}, u32[]{:S(2)}) collective-permute-start(bf16[2,256,2,2,64]{1,0,4,3,2:T(2,128)(2,1)S(1)} %collective-permute-done.4), channel_id=1, source_target_pairs={{0,8},{4,12},{8,16},{12,20},{16,24},{20,28},{24,32},{28,36},{32,40... | collective-permute-start | bytes 786440 | tf_op jit(solution)/shard_map/ppermute | solution.py:19
  381.9 14.1 %collective-permute-start.6 = (bf16[2,256,2,2,64]{1,0,4,3,2:T(2,128)(2,1)S(1)}, bf16[2,256,2,2,64]{1,0,4,3,2:T(2,128)(2,1)S(1)}, u32[]{:S(2)}, u32[]{:S(2)}) collective-permute-start(bf16[2,256,2,2,64]{1,0,4,3,2:T(2,128)(2,1)S(1)} %collective-permute-done.4), channel_id=1, source_target_pairs={{0,4},{4,8},{8,12},{12,16},{16,20},{20,24},{24,28},{28,32},{32,36}... | collective-permute-start | bytes 786440 | tf_op jit(solution)/shard_map/ppermute | solution.py:19
  385.1 2.5 collective-permute-start.7
  387.6 7.9 %collective-permute-start.8 = (s32[2,256]{1,0:T(2,128)S(1)}, s32[2,256]{1,0:T(2,128)S(1)}, u32[]{:S(2)}, u32[]{:S(2)}) collective-permute-start(s32[2,256]{1,0:T(2,128)S(1)} %collective-permute-done.7), channel_id=1, source_target_pairs={{0,8},{4,12},{8,16},{12,20},{16,24},{20,28},{24,32},{28,36},{32,40... | collective-permute-start | bytes 6152 | tf_op jit(solution)/shard_map/ppermute | solution.py:19
  390.6 4.8 collective-permute-start.9
  453.4 58.3 %copy-start.1 = (bf16[512,512]{1,0:T(8,128)(2,1)S(1)}, bf16[512,512]{1,0:T(8,128)(2,1)}, u32[]{:S(2)}) copy-start(bf16[512,512]{1,0:T(8,128)(2,1)} %fusion.110) | copy-start | bytes 1572868
Sparse Core Ops, SparseCore 0:
  9.1 33.3 all-gather.6
  45.1 74.6 all-gather.8
  122.4 73.7 all-gather.10
  201.3 58.0 reduce-scatter.2
  261.8 29.1 all-gather.12
  293.4 74.6 all-gather.14
  374.5 73.8 all-gather.16
  453.5 58.0 reduce-scatter.4
where the time goes:
time: 521 us
  waiting for transfers between devices  408 us (78%)
  matrix products  53.8 us (10%)
  starting transfers between devices  27.2 us (5%)
  between operations  13.8 us (3%)
  other arithmetic  12.2 us (2%)
    all_gather x2, waiting for transfers between devices, project_in(): lax.all_gather(weight_rows, 'tm', axis=0, tiled=True)  150 us
    reduce_scatter x2, waiting for transfers between devices, project_out(): summed = lax.psum_scatter(terms, 'mp', scatter_dimension=1, tiled=True)  116 us
    all_gather x2, waiting for transfers between devices, project_out(): lax.all_gather(weight, 'tm', axis=1, tiled=True)  65.2 us
    all_gather x1, waiting for transfers between devices, body(): full = lax.all_gather(motion, 'mp', axis=3, tiled=True).reshape(count, D)  32.9 us
    all_gather x1, waiting for transfers between devices, body(): hidden_full = lax.all_gather(hidden, 'mp', axis=1, tiled=True)  28.5 us
    sub x4, matrix products, one_clip(): exps = jnp.where(allowed, jnp.exp(scores - top), 0.0)  25.7 us
    ppermute x8, starting transfers between devices, passed_along(): lax.ppermute(value, axis, [(source, source + steps) for source in range(l...  24.2 us
  transfers between devices with their start and end apart: 18, of which 13 were waited for; matrix products, arithmetic and copies ran while one was open for 10% of the time, Pallas kernels for 0%

commit v1 on v0

--- a/solution.py
+++ b/solution.py
@@ -19,10 +19,22 @@
     return lax.ppermute(value, axis, [(source, source + steps) for source in range(leading, last)])
 
 
-def swapped(value, axis, apart):
-    mask = 2**apart
+def swapped(value, axis, mask):
     pairs = [(source, source ^ mask) for source in range(lax.axis_size(axis))]
     return lax.ppermute(value, axis, pairs)
+
+
+def gathered_mp(block):
+    count = lax.axis_size("mp")
+    me = lax.axis_index("mp")
+    width = block.shape[-1]
+    full = jnp.zeros(block.shape[:-1] + (width * count,), block.dtype)
+    zeros = (0,) * (block.ndim - 1)
+    full = lax.dynamic_update_slice(full, block, zeros + (me * width,))
+    for mask in range(1, count):
+        piece = swapped(block, "mp", mask)
+        full = lax.dynamic_update_slice(full, piece, zeros + ((me ^ mask) * width,))
+    return full
 
 
 def rms_normed(rows, gain):
@@ -38,6 +50,27 @@
         preferred_element_type=jnp.float32,
     )
     return total.astype(jnp.bfloat16)
+
+
+def out_weight(weight):
+    count = lax.axis_size("mp")
+    me = lax.axis_index("mp")
+    rows = lax.all_gather(weight, "tm", axis=1, tiled=True)
+    width = rows.shape[1] // count
+    pieces = [lax.dynamic_slice_in_dim(rows, me * width, width, 1)]
+    for mask in range(1, count):
+        part = lax.dynamic_slice_in_dim(rows, (me ^ mask) * width, width, 1)
+        pieces.append(swapped(part, "mp", mask))
+    return jnp.concatenate(pieces, 0)
+
+
+def project_out(heads, weight_pieces, residual):
+    count = lax.axis_size("mp")
+    pieces = [heads] + [swapped(heads, "mp", mask) for mask in range(1, count)]
+    terms = jnp.dot(
+        jnp.concatenate(pieces, 1), weight_pieces, preferred_element_type=jnp.float32
+    )
+    return (residual.astype(jnp.float32) + terms).astype(jnp.bfloat16)
 
 
 def earlier_frames(pair, frames):
@@ -77,14 +110,6 @@
     return outputs.reshape(outputs.shape[0] * outputs.shape[1], -1)
 
 
-def project_out(heads, weight, residual):
-    terms = jnp.dot(
-        heads, lax.all_gather(weight, "tm", axis=1, tiled=True), preferred_element_type=jnp.float32
-    )
-    summed = lax.psum_scatter(terms, "mp", scatter_dimension=1, tiled=True)
-    return (residual.astype(jnp.float32) + summed).astype(jnp.bfloat16)
-
-
 def body(motion, valid, windows, gains, w_self_in, w_self_out, w_cross_in, w_cross_out):
     clips = motion.shape[1]
     frames = motion.shape[2]
@@ -97,7 +122,9 @@
     ).reshape(local_groups, group)
     own_valid = valid[0]
     residual = motion.reshape(count, motion.shape[3])
-    full = lax.all_gather(motion, "mp", axis=3, tiled=True).reshape(count, D)
+    self_out_w = out_weight(w_self_out)
+    cross_out_w = out_weight(w_cross_out)
+    full = gathered_mp(residual)
     normed = rms_normed(full, gains[0])
     self_proj = project_in(normed, w_self_in).reshape(
         clips, frames, local_groups, group + 2, HEAD_DIM
@@ -105,17 +132,17 @@
     self_pair = self_proj[:, :, :, group:]
     key_vals, masks = earlier_frames((self_pair, own_valid), frames)
     self_heads = window_attend(self_proj[:, :, :, :group], key_vals, masks, wins)
-    hidden = project_out(self_heads, w_self_out, residual)
-    hidden_full = lax.all_gather(hidden, "mp", axis=1, tiled=True)
+    hidden = project_out(self_heads, self_out_w, residual)
+    hidden_full = gathered_mp(hidden)
     normed2 = rms_normed(hidden_full, gains[1])
     cross_proj = project_in(normed2, w_cross_in).reshape(
         clips, frames, local_groups, group + 2, HEAD_DIM
     )
     cross_pair = cross_proj[:, :, :, group:]
-    partner = swapped((cross_pair, own_valid), "person", 0)
+    partner = swapped((cross_pair, own_valid), "person", 1)
     partner_vals, partner_masks = earlier_frames(partner, frames)
     cross_heads = window_attend(cross_proj[:, :, :, :group], partner_vals, partner_masks, wins)
-    mixed = project_out(cross_heads, w_cross_out, hidden)
+    mixed = project_out(cross_heads, cross_out_w, hidden)
     return mixed.reshape(motion.shape)
 
 

time: 521 us -> 396 us (0.76)
  waiting for transfers between devices: 408 us -> 251 us
  starting transfers between devices: 27.2 us -> 62.2 us
  local copies, waits for them, and re-layouts: 5.06 us -> 14.5 us
  other arithmetic: 12.2 us -> 3.99 us
    reduce_scatter x2 -> x0, waiting for transfers between devices: 116 us -> none  [project_out(): summed = lax.psum_scatter(terms, 'mp', scatter_dimension=1, tiled=True)]
    all_gather x2, waiting for transfers between devices: 150 us -> 50.1 us  [project_in(): lax.all_gather(weight_rows, 'tm', axis=0, tiled=True)]
    ppermute x2 -> x20, waiting for transfers between devices: 5.22 us -> 87.7 us  [swapped(): return lax.ppermute(value, axis, pairs)]
    ppermute x2 -> x20, starting transfers between devices: 2.53 us -> 36.6 us  [swapped(): return lax.ppermute(value, axis, pairs)]
    all_gather x4 -> x2, waiting for transfers between devices: 127 us -> 111 us  [out_weight(): rows = lax.all_gather(weight, 'tm', axis=1, tiled=True)]
    ppermute x8, waiting for transfers between devices: 7.96 us -> 0.02 us  [passed_along(): lax.ppermute(value, axis, [(source, source + steps) for source in range(l...]
    dynamic_slice x0 -> x2, local copies, waits for them, and re-layouts: none -> 5.8 us  [out_weight(): pieces = [lax.dynamic_slice_in_dim(rows, me * width, width, 1)]]
  transfers between devices with their start and end apart: 18 -> 32, of which waited for: 13 -> 12; matrix products, arithmetic and copies ran while one was open for 10% -> 16% of each run, Pallas kernels for 0% -> 0%
where the time goes in v1:
time: 396 us; the launch traced here: 395 us
  waiting for transfers between devices  251 us (63%)
  starting transfers between devices  62.2 us (16%)
  matrix products  49.6 us (13%)
  local copies, waits for them, and re-layouts  14.5 us (4%)
  between operations  13.7 us (3%)
  other arithmetic  3.99 us (1%)
    all_gather x2, waiting for transfers between devices, out_weight(): rows = lax.all_gather(weight, 'tm', axis=1, tiled=True)  111 us
    ppermute x20, waiting for transfers between devices, swapped(): return lax.ppermute(value, axis, pairs)  87.7 us
    all_gather x2, waiting for transfers between devices, project_in(): lax.all_gather(weight_rows, 'tm', axis=0, tiled=True)  50.1 us
    ppermute x20, starting transfers between devices, swapped(): return lax.ppermute(value, axis, pairs)  36.6 us
    sub x4, matrix products, one_clip(): exps = jnp.where(allowed, jnp.exp(scores - top), 0.0)  25.5 us
    ppermute x8, starting transfers between devices, passed_along(): lax.ppermute(value, axis, [(source, source + steps) for source in range(l...  25.5 us
    dot_general x4, matrix products, one_clip(): jnp.einsum('kgqc,ckd->qkgd', weights, values, preferred_element_type=jnp....  10.2 us
  transfers between devices with their start and end apart: 32, of which 12 were waited for; matrix products, arithmetic and copies ran while one was open for 16% of the time, Pallas kernels for 0%

profile of v1, /device:TPU:1, one launch (start us, length us, event | category | flops | bytes accessed | tf_op | source)
XLA Modules:
  0.0 394.9 jit_solution(1430733067297846508)
XLA Ops:
  8.8 3.3 collective-permute-start
  15.3 3.2 collective-permute-start.5
  18.5 3.5 collective-permute-start.6
  27.2 11.4 %collective-permute-done.2 = bf16[512,512]{1,0:T(8,128)(2,1)S(1)} collective-permute-done((bf16[512,512]{1,0:T(8,128)(2,1)}, bf16[512,512]{1,0:T(8,128)(2,1)S(1)}, u32[]{:S(2)}, u32[]{:S(2)}) %collective-permute-start.2) | collective-permute-done | bytes 524320 | tf_op jit(solution)/shard_map/ppermute | solution.py:24
  39.2 50.1 %all-gather.5.cloned.1.call-done = bf16[2048,768]{1,0:T(8,128)(2,1)} async-done(((bf16[64,768]{1,0:T(8,128)(2,1)}), bf16[2048,768]{1,0:T(8,128)(2,1)}) %all-gather.5.cloned.1.call-update) | async-done | bytes 3145744 | tf_op jit(solution)/shard_map/all_gather | solution.py:49
  89.3 3.7 fusion.142
  93.7 3.5 collective-permute-start.3
  97.2 3.2 collective-permute-start.4
  100.4 65.4 %all-gather.7.cloned.1.call-done = bf16[512,2048]{0,1:T(8,128)(2,1)} async-done(((bf16[512,64]{0,1:T(8,128)(2,1)}), bf16[512,2048]{0,1:T(8,128)(2,1)}) %all-gather.7.cloned.1.call-update) | async-done | bytes 2097168 | tf_op jit(solution)/shard_map/all_gather | solution.py:58
  168.6 5.5 %collective-permute-start.10 = (bf16[512,512]{0,1:T(8,128)(2,1)}, bf16[512,512]{0,1:T(8,128)(2,1)}, u32[]{:S(2)}, u32[]{:S(2)}) collective-permute-start(bf16[512,512]{0,1:T(8,128)(2,1)} %get-tuple-element.222), channel_id=1, source_target_pairs={{0,1},{1,0},{2,3},{3,2},{4,5},{5,4},{6,7},{7,6},{8,9},{9,8},{10,11... | collective-permute-start | bytes 1572872 | tf_op jit(solution)/shard_map/ppermute | solution.py:24
  178.6 19.0 %while.24 = (s32[]{:T(128)}, bf16[2,256,2,4,64]{1,4,3,2,0:T(8,128)(2,1)S(1)}, bf16[2,768,2,2,64]{1,4,2,3,0:T(8,128)(2,1)S(1)}, s32[8]{0:T(128)S(1)}, s32[2,768]{...) while((s32[]{:T(128)}, ...), condition=%wide.region_4.5_spmd.clone.clone, body=%wide.region_1.4_spmd.clone.clone.sunk | while | flops 625673728 | bytes 12019361 | solution.py:109
  179.2 6.4 %fusion.189 = (f32[2,4,256]{2,1,0:T(4,128)S(1)}, bf16[2,4,256,768]{2,3,1,0:T(8,128)(2,1)}) fusion(s32[2,4]{1,0:T(2,128)S(1)} %lt.153, s32[256,768]{0,1:T(8,128)S(1)} %iota_subtract_fusion.4, pred[256,768]{0,1:T(8,128)(4,1)S(1)} %get-tuple-element.318, pred[256,768]{0,1:T(8,128)(4,1)S(1)} %get-tuple-element.319, ...), kind=kOutput, calls=%fused_computation.151.clone.1 | convolution fusion | flops 423101184 | bytes 6433792 | tf_op jit(solution)/shard_map/while/body/eval_jaxpr/sub | solution.py:103
  188.6 6.4 %fusion.189 = (f32[2,4,256]{2,1,0:T(4,128)S(1)}, bf16[2,4,256,768]{2,3,1,0:T(8,128)(2,1)}) fusion(s32[2,4]{1,0:T(2,128)S(1)} %lt.153, s32[256,768]{0,1:T(8,128)S(1)} %iota_subtract_fusion.4, pred[256,768]{0,1:T(8,128)(4,1)S(1)} %get-tuple-element.318, pred[256,768]{0,1:T(8,128)(4,1)S(1)} %get-tuple-element.319, ...), kind=kOutput, calls=%fused_computation.151.clone.1 | convolution fusion | flops 423101184 | bytes 6433792 | tf_op jit(solution)/shard_map/while/body/eval_jaxpr/sub | solution.py:103
  202.0 11.3 %collective-permute-done.8 = bf16[512,512]{0,1:T(8,128)(2,1)S(1)} collective-permute-done((bf16[512,512]{0,1:T(8,128)(2,1)S(1)}, bf16[512,512]{0,1:T(8,128)(2,1)S(1)}, u32[]{:S(2)}, u32[]{:S(2)}) %collective-permute-start.8) | collective-permute-done | bytes 524320 | tf_op jit(solution)/shard_map/ppermute | solution.py:24
  213.3 11.7 %collective-permute-done.9 = bf16[512,512]{0,1:T(8,128)(2,1)S(1)} collective-permute-done((bf16[512,512]{0,1:T(8,128)(2,1)S(1)}, bf16[512,512]{0,1:T(8,128)(2,1)S(1)}, u32[]{:S(2)}, u32[]{:S(2)}) %collective-permute-start.9) | collective-permute-done | bytes 524320 | tf_op jit(solution)/shard_map/ppermute | solution.py:24
  228.1 3.1 collective-permute-start.14
  231.8 11.1 %collective-permute-done.14 = bf16[512,512]{1,0:T(8,128)(2,1)S(1)} collective-permute-done((bf16[512,512]{1,0:T(8,128)(2,1)S(1)}, bf16[512,512]{1,0:T(8,128)(2,1)S(1)}, u32[]{:S(2)}, u32[]{:S(2)}) %collective-permute-start.14) | collective-permute-done | bytes 524320 | tf_op jit(solution)/shard_map/ppermute | solution.py:24
  243.0 11.7 %collective-permute-done.15 = bf16[512,512]{1,0:T(8,128)(2,1)S(1)} collective-permute-done((bf16[512,512]{1,0:T(8,128)(2,1)S(1)}, bf16[512,512]{1,0:T(8,128)(2,1)S(1)}, u32[]{:S(2)}, u32[]{:S(2)}) %collective-permute-start.15) | collective-permute-done | bytes 524320 | tf_op jit(solution)/shard_map/ppermute | solution.py:24
  255.3 3.7 fusion.145
  261.3 6.4 %collective-permute-done.19 = s32[2,256]{1,0:T(2,128)S(1)} collective-permute-done((s32[2,256]{1,0:T(2,128)S(1)}, s32[2,256]{1,0:T(2,128)S(1)}, u32[]{:S(2)}, u32[]{:S(2)}) %collective-permute-start.19) | collective-permute-done | bytes 2080 | tf_op jit(solution)/shard_map/ppermute | solution.py:24
  267.7 3.3 collective-permute-start.20
  273.6 3.1 collective-permute-start.17
  276.7 3.2 collective-permute-start.18
  280.0 45.5 %all-gather.11.cloned.1.call-done = bf16[512,2048]{0,1:T(8,128)(2,1)} async-done(((bf16[512,64]{0,1:T(8,128)(2,1)}), bf16[512,2048]{0,1:T(8,128)(2,1)}) %all-gather.11.cloned.1.call-update) | async-done | bytes 2097168 | tf_op jit(solution)/shard_map/all_gather | solution.py:58
  325.5 2.9 constant_dynamic-slice_fusion.3
  328.4 5.5 %collective-permute-start.25 = (bf16[512,512]{0,1:T(8,128)(2,1)}, bf16[512,512]{0,1:T(8,128)(2,1)}, u32[]{:S(2)}, u32[]{:S(2)}) collective-permute-start(bf16[512,512]{0,1:T(8,128)(2,1)} %get-tuple-element.218), channel_id=1, source_target_pairs={{0,1},{1,0},{2,3},{3,2},{4,5},{5,4},{6,7},{7,6},{8,9},{9,8},{10,11... | collective-permute-start | bytes 1572872 | tf_op jit(solution)/shard_map/ppermute | solution.py:24
  338.4 18.8 %while.25 = (s32[]{:T(128)}, bf16[2,256,2,4,64]{1,4,3,2,0:T(8,128)(2,1)S(1)}, bf16[2,768,2,2,64]{1,4,2,3,0:T(8,128)(2,1)S(1)}, s32[8]{0:T(128)S(1)}, s32[2,768]{...) while((s32[]{:T(128)}, ...), condition=%wide.region_9.10_spmd.clone.clone, body=%wide.region_6.9_spmd.clone.clone.sunk | while | flops 625673728 | bytes 12019361 | solution.py:109
  338.9 6.3 %fusion.195 = (f32[2,4,256]{2,1,0:T(4,128)S(1)}, bf16[2,4,256,768]{2,3,1,0:T(8,128)(2,1)}) fusion(s32[2,4]{1,0:T(2,128)S(1)} %lt.157, s32[256,768]{0,1:T(8,128)S(1)} %iota_subtract_fusion.5, pred[256,768]{0,1:T(8,128)(4,1)S(1)} %get-tuple-element.329, pred[256,768]{0,1:T(8,128)(4,1)S(1)} %get-tuple-element.330, ...), kind=kOutput, calls=%fused_computation.152.clone.1 | convolution fusion | flops 423101184 | bytes 6433792 | tf_op jit(solution)/shard_map/while/body/eval_jaxpr/sub | solution.py:103
  348.4 6.3 %fusion.195 = (f32[2,4,256]{2,1,0:T(4,128)S(1)}, bf16[2,4,256,768]{2,3,1,0:T(8,128)(2,1)}) fusion(s32[2,4]{1,0:T(2,128)S(1)} %lt.157, s32[256,768]{0,1:T(8,128)S(1)} %iota_subtract_fusion.5, pred[256,768]{0,1:T(8,128)(4,1)S(1)} %get-tuple-element.329, pred[256,768]{0,1:T(8,128)(4,1)S(1)} %get-tuple-element.330, ...), kind=kOutput, calls=%fused_computation.152.clone.1 | convolution fusion | flops 423101184 | bytes 6433792 | tf_op jit(solution)/shard_map/while/body/eval_jaxpr/sub | solution.py:103
  361.7 11.3 %collective-permute-done.23 = bf16[512,512]{0,1:T(8,128)(2,1)S(1)} collective-permute-done((bf16[512,512]{0,1:T(8,128)(2,1)S(1)}, bf16[512,512]{0,1:T(8,128)(2,1)S(1)}, u32[]{:S(2)}, u32[]{:S(2)}) %collective-permute-start.23) | collective-permute-done | bytes 524320 | tf_op jit(solution)/shard_map/ppermute | solution.py:24
  372.9 11.7 %collective-permute-done.24 = bf16[512,512]{0,1:T(8,128)(2,1)S(1)} collective-permute-done((bf16[512,512]{0,1:T(8,128)(2,1)S(1)}, bf16[512,512]{0,1:T(8,128)(2,1)S(1)}, u32[]{:S(2)}, u32[]{:S(2)}) %collective-permute-start.24) | collective-permute-done | bytes 524320 | tf_op jit(solution)/shard_map/ppermute | solution.py:24
  384.6 3.8 add_convert_fusion
  (118 shorter events, 53.5 us)
Async XLA Ops:
  6.5 82.8 %all-gather.5.cloned.1.call-start = ((), (), s32[]{:S(2)}) async-start(), calls=%async_computation | async-start | bytes 3244032 | tf_op jit(solution)/shard_map/all_gather | solution.py:49
  7.3 158.5 %all-gather.7.cloned.1.call-start = ((), (), s32[]{:S(2)}) async-start(), calls=%async_computation.1 | async-start | bytes 2162688 | tf_op jit(solution)/shard_map/all_gather | solution.py:58
  8.0 247.3 %all-gather.9.cloned.1.call-start = ((), (), s32[]{:S(2)}) async-start(), calls=%async_computation.2 | async-start | bytes 3244032 | tf_op jit(solution)/shard_map/all_gather | solution.py:49
  8.7 316.8 %all-gather.11.cloned.1.call-start = ((), (), s32[]{:S(2)}) async-start(), calls=%async_computation.3 | async-start | bytes 2162688 | tf_op jit(solution)/shard_map/all_gather | solution.py:58
  8.8 16.2 %collective-permute-start = (bf16[512,512]{1,0:T(8,128)(2,1)}, bf16[512,512]{1,0:T(8,128)(2,1)}, u32[]{:S(2)}, u32[]{:S(2)}) collective-permute-start(bf16[512,512]{1,0:T(8,128)(2,1)} %bitcast.203), channel_id=1, source_target_pairs={{0,1},{1,0},{2,3},{3,2},{4,5},{5,4},{6,7},{7,6},{8,9},{9,8},{10,11... | collective-permute-start | bytes 1572872 | tf_op jit(solution)/shard_map/ppermute | solution.py:24
  12.1 15.1 %collective-permute-start.1 = (bf16[512,512]{1,0:T(8,128)(2,1)}, bf16[512,512]{1,0:T(8,128)(2,1)S(1)}, u32[]{:S(2)}, u32[]{:S(2)}) collective-permute-start(bf16[512,512]{1,0:T(8,128)(2,1)} %bitcast.204), channel_id=1, source_target_pairs={{0,2},{1,3},{2,0},{3,1},{4,6},{5,7},{6,4},{7,5},{8,10},{9,11},{10,... | collective-permute-start | bytes 1572872 | tf_op jit(solution)/shard_map/ppermute | solution.py:24
  13.1 25.6 %collective-permute-start.2 = (bf16[512,512]{1,0:T(8,128)(2,1)}, bf16[512,512]{1,0:T(8,128)(2,1)S(1)}, u32[]{:S(2)}, u32[]{:S(2)}) collective-permute-start(bf16[512,512]{1,0:T(8,128)(2,1)} %bitcast.205), channel_id=1, source_target_pairs={{0,3},{1,2},{2,1},{3,0},{4,7},{5,6},{6,5},{7,4},{8,11},{9,10},{10,... | collective-permute-start | bytes 1572872 | tf_op jit(solution)/shard_map/ppermute | solution.py:24
  15.3 85.0 %collective-permute-start.5 = (s32[2,256]{1,0:T(2,128)}, s32[2,256]{1,0:T(2,128)S(1)}, u32[]{:S(2)}, u32[]{:S(2)}) collective-permute-start(s32[2,256]{1,0:T(2,128)} %bitcast.210), channel_id=1, source_target_pairs={{0,8},{4,12},{8,16},{12,20},{16,24},{20,28},{24,32},{28,36},{32,40... | collective-permute-start | bytes 6152 | tf_op jit(solution)/shard_map/ppermute | solution.py:19
  18.5 81.9 %collective-permute-start.6 = (s32[2,256]{1,0:T(2,128)}, s32[2,256]{1,0:T(2,128)S(1)}, u32[]{:S(2)}, u32[]{:S(2)}) collective-permute-start(s32[2,256]{1,0:T(2,128)} %bitcast.211), channel_id=1, source_target_pairs={{0,4},{4,8},{8,12},{12,16},{16,20},{20,24},{24,28},{28,32},{32,36}... | collective-permute-start | bytes 6152 | tf_op jit(solution)/shard_map/ppermute | solution.py:19
  93.7 84.0 %collective-permute-start.3 = (bf16[2,256,2,2,64]{1,0,4,3,2:T(2,128)(2,1)S(1)}, bf16[2,256,2,2,64]{1,0,4,3,2:T(2,128)(2,1)S(1)}, u32[]{:S(2)}, u32[]{:S(2)}) collective-permute-start(bf16[2,256,2,2,64]{1,0,4,3,2:T(2,128)(2,1)S(1)} %slice.48), channel_id=1, source_target_pairs={{0,8},{4,12},{8,16},{12,20},{16,24},{20,28},{24,32},{28,36},{32,40... | collective-permute-start | bytes 786440 | tf_op jit(solution)/shard_map/ppermute | solution.py:19
  97.2 80.5 %collective-permute-start.4 = (bf16[2,256,2,2,64]{1,0,4,3,2:T(2,128)(2,1)S(1)}, bf16[2,256,2,2,64]{1,0,4,3,2:T(2,128)(2,1)S(1)}, u32[]{:S(2)}, u32[]{:S(2)}) collective-permute-start(bf16[2,256,2,2,64]{1,0,4,3,2:T(2,128)(2,1)S(1)} %slice.48), channel_id=1, source_target_pairs={{0,4},{4,8},{8,12},{12,16},{16,20},{20,24},{24,28},{28,32},{32,36}... | collective-permute-start | bytes 786440 | tf_op jit(solution)/shard_map/ppermute | solution.py:19
  168.6 32.7 %collective-permute-start.10 = (bf16[512,512]{0,1:T(8,128)(2,1)}, bf16[512,512]{0,1:T(8,128)(2,1)}, u32[]{:S(2)}, u32[]{:S(2)}) collective-permute-start(bf16[512,512]{0,1:T(8,128)(2,1)} %get-tuple-element.222), channel_id=1, source_target_pairs={{0,1},{1,0},{2,3},{3,2},{4,5},{5,4},{6,7},{7,6},{8,9},{9,8},{10,11... | collective-permute-start | bytes 1572872 | tf_op jit(solution)/shard_map/ppermute | solution.py:24
  174.1 27.9 %collective-permute-start.11 = (bf16[512,512]{0,1:T(8,128)(2,1)}, bf16[512,512]{0,1:T(8,128)(2,1)}, u32[]{:S(2)}, u32[]{:S(2)}) collective-permute-start(bf16[512,512]{0,1:T(8,128)(2,1)} %get-tuple-element.221), channel_id=1, source_target_pairs={{0,2},{1,3},{2,0},{3,1},{4,6},{5,7},{6,4},{7,5},{8,10},{9,11},{10,... | collective-permute-start | bytes 1572872 | tf_op jit(solution)/shard_map/ppermute | solution.py:24
  176.8 25.2 %collective-permute-start.12 = (bf16[512,512]{0,1:T(8,128)(2,1)}, bf16[512,512]{0,1:T(8,128)(2,1)}, u32[]{:S(2)}, u32[]{:S(2)}) collective-permute-start(bf16[512,512]{0,1:T(8,128)(2,1)} %get-tuple-element.220), channel_id=1, source_target_pairs={{0,3},{1,2},{2,1},{3,0},{4,7},{5,6},{6,5},{7,4},{8,11},{9,10},{10,... | collective-permute-start | bytes 1572872 | tf_op jit(solution)/shard_map/ppermute | solution.py:24
  198.3 3.7 collective-permute-start.7
  198.6 14.7 %collective-permute-start.8 = (bf16[512,512]{0,1:T(8,128)(2,1)S(1)}, bf16[512,512]{0,1:T(8,128)(2,1)S(1)}, u32[]{:S(2)}, u32[]{:S(2)}) collective-permute-start(bf16[512,512]{0,1:T(8,128)(2,1)S(1)} %bitcast.196), channel_id=1, source_target_pairs={{0,2},{1,3},{2,0},{3,1},{4,6},{5,7},{6,4},{7,5},{8,10},{9,11},{10,... | collective-permute-start | bytes 1572872 | tf_op jit(solution)/shard_map/ppermute | solution.py:24
  201.3 23.7 %collective-permute-start.9 = (bf16[512,512]{0,1:T(8,128)(2,1)S(1)}, bf16[512,512]{0,1:T(8,128)(2,1)S(1)}, u32[]{:S(2)}, u32[]{:S(2)}) collective-permute-start(bf16[512,512]{0,1:T(8,128)(2,1)S(1)} %bitcast.197), channel_id=1, source_target_pairs={{0,3},{1,2},{2,1},{3,0},{4,7},{5,6},{6,5},{7,4},{8,11},{9,10},{10,... | collective-permute-start | bytes 1572872 | tf_op jit(solution)/shard_map/ppermute | solution.py:24
  228.0 3.7 collective-permute-start.13
  228.1 14.8 %collective-permute-start.14 = (bf16[512,512]{1,0:T(8,128)(2,1)S(1)}, bf16[512,512]{1,0:T(8,128)(2,1)S(1)}, u32[]{:S(2)}, u32[]{:S(2)}) collective-permute-start(bf16[512,512]{1,0:T(8,128)(2,1)S(1)} %get-tuple-element.226), channel_id=1, source_target_pairs={{0,2},{1,3},{2,0},{3,1},{4,6},{5,7},{6,4},{7,5},{8,10},{9,11},{10,... | collective-permute-start | bytes 1572872 | tf_op jit(solution)/shard_map/ppermute | solution.py:24
  231.3 23.4 %collective-permute-start.15 = (bf16[512,512]{1,0:T(8,128)(2,1)S(1)}, bf16[512,512]{1,0:T(8,128)(2,1)S(1)}, u32[]{:S(2)}, u32[]{:S(2)}) collective-permute-start(bf16[512,512]{1,0:T(8,128)(2,1)S(1)} %get-tuple-element.226), channel_id=1, source_target_pairs={{0,3},{1,2},{2,1},{3,0},{4,7},{5,6},{6,5},{7,4},{8,11},{9,10},{10,... | collective-permute-start | bytes 1572872 | tf_op jit(solution)/shard_map/ppermute | solution.py:24
  259.7 13.9 %collective-permute-start.16 = (bf16[2,256,2,2,64]{1,0,4,3,2:T(2,128)(2,1)S(1)}, bf16[2,256,2,2,64]{1,0,4,3,2:T(2,128)(2,1)S(1)}, u32[]{:S(2)}, u32[]{:S(2)}) collective-permute-start(bf16[2,256,2,2,64]{1,0,4,3,2:T(2,128)(2,1)S(1)} %slice.50), channel_id=1, source_target_pairs={{0,128},{128,0},{1,129},{129,1},{2,130},{130,2},{3,131},{131,3},{4... | collective-permute-start | bytes 786440 | tf_op jit(solution)/shard_map/ppermute | solution.py:24
  261.2 6.5 %collective-permute-start.19 = (s32[2,256]{1,0:T(2,128)S(1)}, s32[2,256]{1,0:T(2,128)S(1)}, u32[]{:S(2)}, u32[]{:S(2)}) collective-permute-start(s32[2,256]{1,0:T(2,128)S(1)} %bitcast.213), channel_id=1, source_target_pairs={{0,128},{128,0},{1,129},{129,1},{2,130},{130,2},{3,131},{131,3},{4... | collective-permute-start | bytes 6152 | tf_op jit(solution)/shard_map/ppermute | solution.py:24
  267.7 12.2 %collective-permute-start.20 = (s32[2,256]{1,0:T(2,128)S(1)}, s32[2,256]{1,0:T(2,128)S(1)}, u32[]{:S(2)}, u32[]{:S(2)}) collective-permute-start(s32[2,256]{1,0:T(2,128)S(1)} %collective-permute-done.19), channel_id=1, source_target_pairs={{0,8},{4,12},{8,16},{12,20},{16,24},{20,28},{24,32},{28,36},{32,40... | collective-permute-start | bytes 6152 | tf_op jit(solution)/shard_map/ppermute | solution.py:19
  271.0 8.9 %collective-permute-start.21 = (s32[2,256]{1,0:T(2,128)S(1)}, s32[2,256]{1,0:T(2,128)S(1)}, u32[]{:S(2)}, u32[]{:S(2)}) collective-permute-start(s32[2,256]{1,0:T(2,128)S(1)} %collective-permute-done.19), channel_id=1, source_target_pairs={{0,4},{4,8},{8,12},{12,16},{16,20},{20,24},{24,28},{28,32},{32,36}... | collective-permute-start | bytes 6152 | tf_op jit(solution)/shard_map/ppermute | solution.py:19
  273.6 63.9 %collective-permute-start.17 = (bf16[2,256,2,2,64]{1,0,4,3,2:T(2,128)(2,1)S(1)}, bf16[2,256,2,2,64]{1,0,4,3,2:T(2,128)(2,1)S(1)}, u32[]{:S(2)}, u32[]{:S(2)}) collective-permute-start(bf16[2,256,2,2,64]{1,0,4,3,2:T(2,128)(2,1)S(1)} %collective-permute-done.16), channel_id=1, source_target_pairs={{0,8},{4,12},{8,16},{12,20},{16,24},{20,28},{24,32},{28,36},{32,40... | collective-permute-start | bytes 786440 | tf_op jit(solution)/shard_map/ppermute | solution.py:19
  276.7 60.8 %collective-permute-start.18 = (bf16[2,256,2,2,64]{1,0,4,3,2:T(2,128)(2,1)S(1)}, bf16[2,256,2,2,64]{1,0,4,3,2:T(2,128)(2,1)S(1)}, u32[]{:S(2)}, u32[]{:S(2)}) collective-permute-start(bf16[2,256,2,2,64]{1,0,4,3,2:T(2,128)(2,1)S(1)} %collective-permute-done.16), channel_id=1, source_target_pairs={{0,4},{4,8},{8,12},{12,16},{16,20},{20,24},{24,28},{28,32},{32,36}... | collective-permute-start | bytes 786440 | tf_op jit(solution)/shard_map/ppermute | solution.py:19
  328.4 32.5 %collective-permute-start.25 = (bf16[512,512]{0,1:T(8,128)(2,1)}, bf16[512,512]{0,1:T(8,128)(2,1)}, u32[]{:S(2)}, u32[]{:S(2)}) collective-permute-start(bf16[512,512]{0,1:T(8,128)(2,1)} %get-tuple-element.218), channel_id=1, source_target_pairs={{0,1},{1,0},{2,3},{3,2},{4,5},{5,4},{6,7},{7,6},{8,9},{9,8},{10,11... | collective-permute-start | bytes 1572872 | tf_op jit(solution)/shard_map/ppermute | solution.py:24
  333.9 27.8 %collective-permute-start.26 = (bf16[512,512]{0,1:T(8,128)(2,1)}, bf16[512,512]{0,1:T(8,128)(2,1)}, u32[]{:S(2)}, u32[]{:S(2)}) collective-permute-start(bf16[512,512]{0,1:T(8,128)(2,1)} %get-tuple-element.217), channel_id=1, source_target_pairs={{0,2},{1,3},{2,0},{3,1},{4,6},{5,7},{6,4},{7,5},{8,10},{9,11},{10,... | collective-permute-start | bytes 1572872 | tf_op jit(solution)/shard_map/ppermute | solution.py:24
  336.6 25.1 %collective-permute-start.27 = (bf16[512,512]{0,1:T(8,128)(2,1)}, bf16[512,512]{0,1:T(8,128)(2,1)}, u32[]{:S(2)}, u32[]{:S(2)}) collective-permute-start(bf16[512,512]{0,1:T(8,128)(2,1)} %get-tuple-element.216), channel_id=1, source_target_pairs={{0,3},{1,2},{2,1},{3,0},{4,7},{5,6},{6,5},{7,4},{8,11},{9,10},{10,... | collective-permute-start | bytes 1572872 | tf_op jit(solution)/shard_map/ppermute | solution.py:24
  357.9 3.7 collective-permute-start.22
  358.2 14.7 %collective-permute-start.23 = (bf16[512,512]{0,1:T(8,128)(2,1)S(1)}, bf16[512,512]{0,1:T(8,128)(2,1)S(1)}, u32[]{:S(2)}, u32[]{:S(2)}) collective-permute-start(bf16[512,512]{0,1:T(8,128)(2,1)S(1)} %bitcast.200), channel_id=1, source_target_pairs={{0,2},{1,3},{2,0},{3,1},{4,6},{5,7},{6,4},{7,5},{8,10},{9,11},{10,... | collective-permute-start | bytes 1572872 | tf_op jit(solution)/shard_map/ppermute | solution.py:24
  360.9 23.7 %collective-permute-start.24 = (bf16[512,512]{0,1:T(8,128)(2,1)S(1)}, bf16[512,512]{0,1:T(8,128)(2,1)S(1)}, u32[]{:S(2)}, u32[]{:S(2)}) collective-permute-start(bf16[512,512]{0,1:T(8,128)(2,1)S(1)} %bitcast.201), channel_id=1, source_target_pairs={{0,3},{1,2},{2,1},{3,0},{4,7},{5,6},{6,5},{7,4},{8,11},{9,10},{10,... | collective-permute-start | bytes 1572872 | tf_op jit(solution)/shard_map/ppermute | solution.py:24
  (4 other events, 89.4 us)
Sparse Core Ops, SparseCore 0:
  9.9 79.3 all-gather.4
  91.9 73.7 all-gather.6
  168.3 77.5 all-gather.8
  248.3 77.1 all-gather.10

commit v2 on v1

--- a/solution.py
+++ b/solution.py
@@ -43,10 +43,24 @@
     return (values * scale * gain).astype(jnp.bfloat16)
 
 
+def split_gather(weight, axis, gather_axis):
+    me = lax.axis_index("person")
+    half = weight.shape[axis] // 2
+    own = lax.all_gather(
+        lax.dynamic_slice_in_dim(weight, me * half, half, axis), "tm", axis=gather_axis, tiled=True
+    )
+    other = swapped(own, "person", 1)
+    shape = list(own.shape)
+    shape[axis] *= 2
+    full = jnp.zeros(shape, own.dtype)
+    full = lax.dynamic_update_slice_in_dim(full, own, me * half, axis)
+    return lax.dynamic_update_slice_in_dim(full, other, (1 - me) * half, axis)
+
+
 def project_in(normed_rows, weight_rows):
     total = jnp.dot(
         normed_rows,
-        lax.all_gather(weight_rows, "tm", axis=0, tiled=True),
+        split_gather(weight_rows, 1, 0),
         preferred_element_type=jnp.float32,
     )
     return total.astype(jnp.bfloat16)
@@ -55,7 +69,7 @@
 def out_weight(weight):
     count = lax.axis_size("mp")
     me = lax.axis_index("mp")
-    rows = lax.all_gather(weight, "tm", axis=1, tiled=True)
+    rows = split_gather(weight, 0, 1)
     width = rows.shape[1] // count
     pieces = [lax.dynamic_slice_in_dim(rows, me * width, width, 1)]
     for mask in range(1, count):

time: 396 us -> 466 us (1.18)
  waiting for transfers between devices: 251 us -> 278 us
  local copies, waits for them, and re-layouts: 14.5 us -> 41 us
  starting transfers between devices: 62.2 us -> 73.4 us
    all_gather x4, waiting for transfers between devices: 161 us -> 203 us  [split_gather(): lax.all_gather(lax.dynamic_slice_in_dim(weight, me * half, half, axis), '...]
    ppermute x20 -> x24, waiting for transfers between devices: 87.7 us -> 67.7 us  [swapped(): return lax.ppermute(value, axis, pairs)]
    dynamic_update_slice x0 -> x8, local copies, waits for them, and re-layouts: none -> 9.73 us  [the longest x4 6.85 us: split_gather(): return lax.dynamic_update_slice_in_dim(full, other, (1 - me) * half, axis)]
    ppermute x20 -> x24, starting transfers between devices: 36.6 us -> 45.3 us  [swapped(): return lax.ppermute(value, axis, pairs)]
    ppermute x8, waiting for transfers between devices: 0.02 us -> 7.16 us  [passed_along(): lax.ppermute(value, axis, [(source, source + steps) for source in range(l...]
    dynamic_slice x0 -> x4, local copies, waits for them, and re-layouts: none -> 4.8 us  [split_gather(): lax.dynamic_slice_in_dim(weight, me * half, half, axis)]
  transfers between devices with their start and end apart: 32 -> 36, of which waited for: 12 -> 12; matrix products, arithmetic and copies ran while one was open for 16% -> 19% of each run, Pallas kernels for 0% -> 0%
where the time goes in v2:
time: 466 us; the launch traced here: 462 us
  waiting for transfers between devices  278 us (60%)
  starting transfers between devices  73.4 us (16%)
  matrix products  50.9 us (11%)
  local copies, waits for them, and re-layouts  41 us (9%)
  between operations  13.7 us (3%)
  other arithmetic  4.86 us (1%)
    all_gather x4, waiting for transfers between devices, split_gather(): lax.all_gather(lax.dynamic_slice_in_dim(weight, me * half, half, axis), '...  203 us
    ppermute x24, waiting for transfers between devices, swapped(): return lax.ppermute(value, axis, pairs)  67.7 us
    ppermute x24, starting transfers between devices, swapped(): return lax.ppermute(value, axis, pairs)  45.3 us
    ppermute x8, starting transfers between devices, passed_along(): lax.ppermute(value, axis, [(source, source + steps) for source in range(l...  27.9 us
    sub x4, matrix products, one_clip(): exps = jnp.where(allowed, jnp.exp(scores - top), 0.0)  25.3 us
    dot_general x4, matrix products, one_clip(): jnp.einsum('kgqc,ckd->qkgd', weights, values, preferred_element_type=jnp....  10.2 us
  transfers between devices with their start and end apart: 36, of which 12 were waited for; matrix products, arithmetic and copies ran while one was open for 19% of the time, Pallas kernels for 0%

profile of v2, /device:TPU:1, one launch (start us, length us, event | category | flops | bytes accessed | tf_op | source)
XLA Modules:
  0.0 462.0 jit_solution(10840410708804077098)
XLA Ops:
  11.1 3.3 collective-permute-start
  17.6 3.2 collective-permute-start.6
  20.8 3.5 collective-permute-start.7
  26.9 59.3 %all-gather.5.cloned.1.call-done = bf16[2048,384]{1,0:T(8,128)(2,1)} async-done(((bf16[64,384]{1,0:T(8,128)(2,1)}), bf16[2048,384]{1,0:T(8,128)(2,1)}) %all-gather.5.cloned.1.call-update) | async-done | bytes 1572880 | tf_op jit(solution)/shard_map/all_gather | solution.py:49
  90.1 72.0 %all-gather.7.cloned.1.call-done = bf16[256,2048]{0,1:T(8,128)(2,1)} async-done(((bf16[256,64]{0,1:T(8,128)(2,1)}), bf16[256,2048]{0,1:T(8,128)(2,1)}) %all-gather.7.cloned.1.call-update) | async-done | bytes 1048592 | tf_op jit(solution)/shard_map/all_gather | solution.py:49
  167.9 71.8 %all-gather.9.cloned.1.call-done = bf16[2048,384]{1,0:T(8,128)(2,1)} async-done(((bf16[64,384]{1,0:T(8,128)(2,1)}), bf16[2048,384]{1,0:T(8,128)(2,1)}) %all-gather.9.cloned.1.call-update) | async-done | bytes 1572880 | tf_op jit(solution)/shard_map/all_gather | solution.py:49
  247.4 4.6 %fusion.142 = bf16[512,768]{1,0:T(8,128)(2,1)} fusion(bf16[2048,768]{1,0:T(8,128)(2,1)} %constant_dynamic-update-slice_fusion.10, bf16[512,2048]{1,0:T(8,128)(2,1)S(1)} %constant_dynamic-update-slice_fusion.12, f32[2048]{0:T(1024)S(1)} %bitcast.209, f32[512]{0:T(512)S(1)} %add_rsqrt_fusion.1), kind=kOutput, calls=%fused_computation.122 | convolution fusion | flops 1615200256 | bytes 6039552 | tf_op jit(solution)/shard_map/dot_general | solution.py:61
  253.8 3.3 collective-permute-start.4
  260.7 2.9 constant_dynamic-slice_fusion.9
  263.6 6.3 %collective-permute-start.12 = (bf16[512,512]{1,0:T(8,128)(2,1)}, bf16[512,512]{1,0:T(8,128)(2,1)}, u32[]{:S(2)}, u32[]{:S(2)}) collective-permute-start(bf16[512,512]{1,0:T(8,128)(2,1)} %get-tuple-element.222), channel_id=1, source_target_pairs={{0,1},{1,0},{2,3},{3,2},{4,5},{5,4},{6,7},{7,6},{8,9},{9,8},{10,11... | collective-permute-start | bytes 1572872 | tf_op jit(solution)/shard_map/ppermute | solution.py:24
  272.8 5.5 %collective-permute-start.14 = (bf16[512,512]{1,0:T(8,128)(2,1)}, bf16[512,512]{1,0:T(8,128)(2,1)}, u32[]{:S(2)}, u32[]{:S(2)}) collective-permute-start(bf16[512,512]{1,0:T(8,128)(2,1)} %get-tuple-element.220), channel_id=1, source_target_pairs={{0,3},{1,2},{2,1},{3,0},{4,7},{5,6},{6,5},{7,4},{8,11},{9,10},{10,... | collective-permute-start | bytes 1572872 | tf_op jit(solution)/shard_map/ppermute | solution.py:24
  279.2 18.8 %while.24 = (s32[]{:T(128)}, bf16[2,256,2,4,64]{1,4,3,2,0:T(8,128)(2,1)S(1)}, bf16[2,768,2,2,64]{1,4,2,3,0:T(8,128)(2,1)S(1)}, s32[8]{0:T(128)S(1)}, s32[2,768]{...) while((s32[]{:T(128)}, ...), condition=%wide.region_4.5_spmd.clone.clone, body=%wide.region_1.4_spmd.clone.clone.sunk | while | flops 625673728 | bytes 12019361 | solution.py:123
  279.7 6.3 %fusion.189 = (f32[2,4,256]{2,1,0:T(4,128)S(1)}, bf16[2,4,256,768]{2,3,1,0:T(8,128)(2,1)}) fusion(s32[2,4]{1,0:T(2,128)S(1)} %lt.177, s32[256,768]{0,1:T(8,128)S(1)} %iota_subtract_fusion.4, pred[256,768]{0,1:T(8,128)(4,1)S(1)} %get-tuple-element.318, pred[256,768]{0,1:T(8,128)(4,1)S(1)} %get-tuple-element.319, ...), kind=kOutput, calls=%fused_computation.163.clone.1 | convolution fusion | flops 423101184 | bytes 6433792 | tf_op jit(solution)/shard_map/while/body/eval_jaxpr/sub | solution.py:117
  289.1 6.3 %fusion.189 = (f32[2,4,256]{2,1,0:T(4,128)S(1)}, bf16[2,4,256,768]{2,3,1,0:T(8,128)(2,1)}) fusion(s32[2,4]{1,0:T(2,128)S(1)} %lt.177, s32[256,768]{0,1:T(8,128)S(1)} %iota_subtract_fusion.4, pred[256,768]{0,1:T(8,128)(4,1)S(1)} %get-tuple-element.318, pred[256,768]{0,1:T(8,128)(4,1)S(1)} %get-tuple-element.319, ...), kind=kOutput, calls=%fused_computation.163.clone.1 | convolution fusion | flops 423101184 | bytes 6433792 | tf_op jit(solution)/shard_map/while/body/eval_jaxpr/sub | solution.py:117
  302.2 4.5 collective-permute-start.23
  306.6 7.9 %collective-permute-done.10 = bf16[512,512]{0,1:T(8,128)(2,1)S(1)} collective-permute-done((bf16[512,512]{0,1:T(8,128)(2,1)S(1)}, bf16[512,512]{0,1:T(8,128)(2,1)S(1)}, u32[]{:S(2)}, u32[]{:S(2)}) %collective-permute-start.10) | collective-permute-done | bytes 524320 | tf_op jit(solution)/shard_map/ppermute | solution.py:24
  314.5 6.6 %collective-permute-done.9 = bf16[512,512]{0,1:T(8,128)(2,1)S(1)} collective-permute-done((bf16[512,512]{0,1:T(8,128)(2,1)S(1)}, bf16[512,512]{0,1:T(8,128)(2,1)S(1)}, u32[]{:S(2)}, u32[]{:S(2)}) %collective-permute-start.9) | collective-permute-done | bytes 524320 | tf_op jit(solution)/shard_map/ppermute | solution.py:24
  321.4 3.4 constant_dynamic-update-slice_fusion.7
  333.8 3.5 collective-permute-start.24
  342.7 11.8 %collective-permute-done.17 = bf16[512,512]{1,0:T(8,128)(2,1)S(1)} collective-permute-done((bf16[512,512]{1,0:T(8,128)(2,1)}, bf16[512,512]{1,0:T(8,128)(2,1)S(1)}, u32[]{:S(2)}, u32[]{:S(2)}) %collective-permute-start.17) | collective-permute-done | bytes 524320 | tf_op jit(solution)/shard_map/ppermute | solution.py:24
  355.1 3.7 fusion.145
  362.1 13.9 %collective-permute-done.28 = bf16[256,2048]{0,1:T(8,128)(2,1)} collective-permute-done((bf16[256,2048]{0,1:T(8,128)(2,1)}, bf16[256,2048]{0,1:T(8,128)(2,1)}, u32[]{:S(2)}, u32[]{:S(2)}) %collective-permute-start.28) | collective-permute-done | bytes 1048608 | tf_op jit(solution)/shard_map/ppermute | solution.py:24
  377.5 4.1 collective-permute-done.19
  381.6 4.4 collective-permute-start.20
  386.0 3.1 collective-permute-start.21
  395.3 7.1 %collective-permute-done.21 = bf16[2,256,2,2,64]{1,0,4,3,2:T(2,128)(2,1)S(1)} collective-permute-done((bf16[2,256,2,2,64]{1,0,4,3,2:T(2,128)(2,1)}, bf16[2,256,2,2,64]{1,0,4,3,2:T(2,128)(2,1)S(1)}, u32[]{:S(2)}, u32[]{:S(2)}) %collective-permute-start.21) | collective-permute-done | bytes 262176 | tf_op jit(solution)/shard_map/ppermute | solution.py:19
  404.2 18.8 %while.25 = (s32[]{:T(128)}, bf16[2,256,2,4,64]{1,4,3,2,0:T(8,128)(2,1)S(1)}, bf16[2,768,2,2,64]{1,4,2,3,0:T(8,128)(2,1)S(1)}, s32[8]{0:T(128)S(1)}, s32[2,768]{...) while((s32[]{:T(128)}, ...), condition=%wide.region_9.10_spmd.clone.clone, body=%wide.region_6.9_spmd.clone.clone.sunk | while | flops 625673728 | bytes 12019361 | solution.py:123
  404.8 6.3 %fusion.195 = (f32[2,4,256]{2,1,0:T(4,128)S(1)}, bf16[2,4,256,768]{2,3,1,0:T(8,128)(2,1)}) fusion(s32[2,4]{1,0:T(2,128)S(1)} %lt.181, s32[256,768]{0,1:T(8,128)S(1)} %iota_subtract_fusion.5, pred[256,768]{0,1:T(8,128)(4,1)S(1)} %get-tuple-element.329, pred[256,768]{0,1:T(8,128)(4,1)S(1)} %get-tuple-element.330, ...), kind=kOutput, calls=%fused_computation.164.clone.1 | convolution fusion | flops 423101184 | bytes 6433792 | tf_op jit(solution)/shard_map/while/body/eval_jaxpr/sub | solution.py:117
  414.2 6.3 %fusion.195 = (f32[2,4,256]{2,1,0:T(4,128)S(1)}, bf16[2,4,256,768]{2,3,1,0:T(8,128)(2,1)}) fusion(s32[2,4]{1,0:T(2,128)S(1)} %lt.181, s32[256,768]{0,1:T(8,128)S(1)} %iota_subtract_fusion.5, pred[256,768]{0,1:T(8,128)(4,1)S(1)} %get-tuple-element.329, pred[256,768]{0,1:T(8,128)(4,1)S(1)} %get-tuple-element.330, ...), kind=kOutput, calls=%fused_computation.164.clone.1 | convolution fusion | flops 423101184 | bytes 6433792 | tf_op jit(solution)/shard_map/while/body/eval_jaxpr/sub | solution.py:117
  428.7 11.6 %collective-permute-done.26 = bf16[512,512]{0,1:T(8,128)(2,1)S(1)} collective-permute-done((bf16[512,512]{0,1:T(8,128)(2,1)S(1)}, bf16[512,512]{0,1:T(8,128)(2,1)S(1)}, u32[]{:S(2)}, u32[]{:S(2)}) %collective-permute-start.26) | collective-permute-done | bytes 524320 | tf_op jit(solution)/shard_map/ppermute | solution.py:24
  440.3 11.5 %collective-permute-done.27 = bf16[512,512]{0,1:T(8,128)(2,1)S(1)} collective-permute-done((bf16[512,512]{0,1:T(8,128)(2,1)S(1)}, bf16[512,512]{0,1:T(8,128)(2,1)S(1)}, u32[]{:S(2)}, u32[]{:S(2)}) %collective-permute-start.27) | collective-permute-done | bytes 524320 | tf_op jit(solution)/shard_map/ppermute | solution.py:24
  451.9 3.6 add_convert_fusion
  (163 shorter events, 86.4 us)
Async XLA Ops:
  6.5 79.7 %all-gather.5.cloned.1.call-start = ((), (), s32[]{:S(2)}) async-start(), calls=%async_computation | async-start | bytes 1622016 | tf_op jit(solution)/shard_map/all_gather | solution.py:49
  8.1 153.9 %all-gather.7.cloned.1.call-start = ((), (), s32[]{:S(2)}) async-start(), calls=%async_computation.1 | async-start | bytes 1081344 | tf_op jit(solution)/shard_map/all_gather | solution.py:49
  9.5 230.1 %all-gather.9.cloned.1.call-start = ((), (), s32[]{:S(2)}) async-start(), calls=%async_computation.2 | async-start | bytes 1622016 | tf_op jit(solution)/shard_map/all_gather | solution.py:49
  11.0 329.1 %all-gather.11.cloned.1.call-start = ((), (), s32[]{:S(2)}) async-start(), calls=%async_computation.3 | async-start | bytes 1081344 | tf_op jit(solution)/shard_map/all_gather | solution.py:49
  11.1 76.7 %collective-permute-start = (bf16[512,512]{1,0:T(8,128)(2,1)}, bf16[512,512]{1,0:T(8,128)(2,1)}, u32[]{:S(2)}, u32[]{:S(2)}) collective-permute-start(bf16[512,512]{1,0:T(8,128)(2,1)} %bitcast.203), channel_id=1, source_target_pairs={{0,1},{1,0},{2,3},{3,2},{4,5},{5,4},{6,7},{7,6},{8,9},{9,8},{10,11... | collective-permute-start | bytes 1572872 | tf_op jit(solution)/shard_map/ppermute | solution.py:24
  14.4 74.6 %collective-permute-start.1 = (bf16[512,512]{1,0:T(8,128)(2,1)}, bf16[512,512]{1,0:T(8,128)(2,1)}, u32[]{:S(2)}, u32[]{:S(2)}) collective-permute-start(bf16[512,512]{1,0:T(8,128)(2,1)} %bitcast.204), channel_id=1, source_target_pairs={{0,2},{1,3},{2,0},{3,1},{4,6},{5,7},{6,4},{7,5},{8,10},{9,11},{10,... | collective-permute-start | bytes 1572872 | tf_op jit(solution)/shard_map/ppermute | solution.py:24
  15.4 147.8 %collective-permute-start.2 = (bf16[512,512]{1,0:T(8,128)(2,1)}, bf16[512,512]{1,0:T(8,128)(2,1)S(1)}, u32[]{:S(2)}, u32[]{:S(2)}) collective-permute-start(bf16[512,512]{1,0:T(8,128)(2,1)} %bitcast.205), channel_id=1, source_target_pairs={{0,3},{1,2},{2,1},{3,0},{4,7},{5,6},{6,5},{7,4},{8,11},{9,10},{10,... | collective-permute-start | bytes 1572872 | tf_op jit(solution)/shard_map/ppermute | solution.py:24
  20.8 66.7 %collective-permute-start.7 = (s32[2,256]{1,0:T(2,128)}, s32[2,256]{1,0:T(2,128)S(1)}, u32[]{:S(2)}, u32[]{:S(2)}) collective-permute-start(s32[2,256]{1,0:T(2,128)} %bitcast.211), channel_id=1, source_target_pairs={{0,4},{4,8},{8,12},{12,16},{16,20},{20,24},{24,28},{28,32},{32,36}... | collective-permute-start | bytes 6152 | tf_op jit(solution)/shard_map/ppermute | solution.py:19
  86.2 158.3 %collective-permute-start.3 = (bf16[2048,384]{1,0:T(8,128)(2,1)}, bf16[2048,384]{1,0:T(8,128)(2,1)}, u32[]{:S(2)}, u32[]{:S(2)}) collective-permute-start(bf16[2048,384]{1,0:T(8,128)(2,1)} %all-gather.5.cloned.1.call-done), channel_id=1, source_target_pairs={{0,128},{128,0},{1,129},{129,1},{2,130},{130,2},{3,131},{131,3},{4... | collective-permute-start | bytes 4718600 | tf_op jit(solution)/shard_map/ppermute | solution.py:24
  87.5 211.2 %collective-permute-start.22 = (s32[2,256]{1,0:T(2,128)S(1)}, s32[2,256]{1,0:T(2,128)S(1)}, u32[]{:S(2)}, u32[]{:S(2)}) collective-permute-start(s32[2,256]{1,0:T(2,128)S(1)} %bitcast.212), channel_id=1, source_target_pairs={{0,128},{128,0},{1,129},{129,1},{2,130},{130,2},{3,131},{131,3},{4... | collective-permute-start | bytes 6152 | tf_op jit(solution)/shard_map/ppermute | solution.py:24
  162.0 81.0 %collective-permute-start.11 = (bf16[256,2048]{0,1:T(8,128)(2,1)}, bf16[256,2048]{0,1:T(8,128)(2,1)}, u32[]{:S(2)}, u32[]{:S(2)}) collective-permute-start(bf16[256,2048]{0,1:T(8,128)(2,1)} %all-gather.7.cloned.1.call-done), channel_id=1, source_target_pairs={{0,128},{128,0},{1,129},{129,1},{2,130},{130,2},{3,131},{131,3},{4... | collective-permute-start | bytes 3145736 | tf_op jit(solution)/shard_map/ppermute | solution.py:24
  239.7 94.2 %collective-permute-start.18 = (bf16[2048,384]{1,0:T(8,128)(2,1)}, bf16[2048,384]{1,0:T(8,128)(2,1)}, u32[]{:S(2)}, u32[]{:S(2)}) collective-permute-start(bf16[2048,384]{1,0:T(8,128)(2,1)} %all-gather.9.cloned.1.call-done), channel_id=1, source_target_pairs={{0,128},{128,0},{1,129},{129,1},{2,130},{130,2},{3,131},{131,3},{4... | collective-permute-start | bytes 4718600 | tf_op jit(solution)/shard_map/ppermute | solution.py:24
  253.8 16.5 %collective-permute-start.4 = (bf16[2,256,2,2,64]{1,0,4,3,2:T(2,128)(2,1)S(1)}, bf16[2,256,2,2,64]{1,0,4,3,2:T(2,128)(2,1)S(1)}, u32[]{:S(2)}, u32[]{:S(2)}) collective-permute-start(bf16[2,256,2,2,64]{1,0,4,3,2:T(2,128)(2,1)S(1)} %slice.48), channel_id=1, source_target_pairs={{0,8},{4,12},{8,16},{12,20},{16,24},{20,28},{24,32},{28,36},{32,40... | collective-permute-start | bytes 786440 | tf_op jit(solution)/shard_map/ppermute | solution.py:19
  257.1 15.7 %collective-permute-start.5 = (bf16[2,256,2,2,64]{1,0,4,3,2:T(2,128)(2,1)S(1)}, bf16[2,256,2,2,64]{1,0,4,3,2:T(2,128)(2,1)S(1)}, u32[]{:S(2)}, u32[]{:S(2)}) collective-permute-start(bf16[2,256,2,2,64]{1,0,4,3,2:T(2,128)(2,1)S(1)} %slice.48), channel_id=1, source_target_pairs={{0,4},{4,8},{8,12},{12,16},{16,20},{20,24},{24,28},{28,32},{32,36}... | collective-permute-start | bytes 786440 | tf_op jit(solution)/shard_map/ppermute | solution.py:19
  263.6 35.3 %collective-permute-start.12 = (bf16[512,512]{1,0:T(8,128)(2,1)}, bf16[512,512]{1,0:T(8,128)(2,1)}, u32[]{:S(2)}, u32[]{:S(2)}) collective-permute-start(bf16[512,512]{1,0:T(8,128)(2,1)} %get-tuple-element.222), channel_id=1, source_target_pairs={{0,1},{1,0},{2,3},{3,2},{4,5},{5,4},{6,7},{7,6},{8,9},{9,8},{10,11... | collective-permute-start | bytes 1572872 | tf_op jit(solution)/shard_map/ppermute | solution.py:24
  270.3 29.0 %collective-permute-start.13 = (bf16[512,512]{1,0:T(8,128)(2,1)}, bf16[512,512]{1,0:T(8,128)(2,1)}, u32[]{:S(2)}, u32[]{:S(2)}) collective-permute-start(bf16[512,512]{1,0:T(8,128)(2,1)} %get-tuple-element.221), channel_id=1, source_target_pairs={{0,2},{1,3},{2,0},{3,1},{4,6},{5,7},{6,4},{7,5},{8,10},{9,11},{10,... | collective-permute-start | bytes 1572872 | tf_op jit(solution)/shard_map/ppermute | solution.py:24
  272.8 29.3 %collective-permute-start.14 = (bf16[512,512]{1,0:T(8,128)(2,1)}, bf16[512,512]{1,0:T(8,128)(2,1)}, u32[]{:S(2)}, u32[]{:S(2)}) collective-permute-start(bf16[512,512]{1,0:T(8,128)(2,1)} %get-tuple-element.220), channel_id=1, source_target_pairs={{0,3},{1,2},{2,1},{3,0},{4,7},{5,6},{6,5},{7,4},{8,11},{9,10},{10,... | collective-permute-start | bytes 1572872 | tf_op jit(solution)/shard_map/ppermute | solution.py:24
  298.7 15.8 %collective-permute-start.10 = (bf16[512,512]{0,1:T(8,128)(2,1)S(1)}, bf16[512,512]{0,1:T(8,128)(2,1)S(1)}, u32[]{:S(2)}, u32[]{:S(2)}) collective-permute-start(bf16[512,512]{0,1:T(8,128)(2,1)S(1)} %bitcast.195), channel_id=1, source_target_pairs={{0,3},{1,2},{2,1},{3,0},{4,7},{5,6},{6,5},{7,4},{8,11},{9,10},{10,... | collective-permute-start | bytes 1572872 | tf_op jit(solution)/shard_map/ppermute | solution.py:24
  298.9 15.7 %collective-permute-start.8 = (bf16[512,512]{0,1:T(8,128)(2,1)S(1)}, bf16[512,512]{0,1:T(8,128)(2,1)S(1)}, u32[]{:S(2)}, u32[]{:S(2)}) collective-permute-start(bf16[512,512]{0,1:T(8,128)(2,1)S(1)} %bitcast.196), channel_id=1, source_target_pairs={{0,1},{1,0},{2,3},{3,2},{4,5},{5,4},{6,7},{7,6},{8,9},{9,8},{10,11... | collective-permute-start | bytes 1572872 | tf_op jit(solution)/shard_map/ppermute | solution.py:24
  299.4 21.8 %collective-permute-start.9 = (bf16[512,512]{0,1:T(8,128)(2,1)S(1)}, bf16[512,512]{0,1:T(8,128)(2,1)S(1)}, u32[]{:S(2)}, u32[]{:S(2)}) collective-permute-start(bf16[512,512]{0,1:T(8,128)(2,1)S(1)} %bitcast.197), channel_id=1, source_target_pairs={{0,2},{1,3},{2,0},{3,1},{4,6},{5,7},{6,4},{7,5},{8,10},{9,11},{10,... | collective-permute-start | bytes 1572872 | tf_op jit(solution)/shard_map/ppermute | solution.py:24
  302.2 58.0 %collective-permute-start.23 = (s32[2,256]{1,0:T(2,128)S(1)}, s32[2,256]{1,0:T(2,128)S(1)}, u32[]{:S(2)}, u32[]{:S(2)}) collective-permute-start(s32[2,256]{1,0:T(2,128)S(1)} %collective-permute-done.22), channel_id=1, source_target_pairs={{0,8},{4,12},{8,16},{12,20},{16,24},{20,28},{24,32},{28,36},{32,40... | collective-permute-start | bytes 6152 | tf_op jit(solution)/shard_map/ppermute | solution.py:19
  324.9 15.3 %collective-permute-start.15 = (bf16[512,512]{1,0:T(8,128)(2,1)}, bf16[512,512]{1,0:T(8,128)(2,1)}, u32[]{:S(2)}, u32[]{:S(2)}) collective-permute-start(bf16[512,512]{1,0:T(8,128)(2,1)} %get-tuple-element.226), channel_id=1, source_target_pairs={{0,1},{1,0},{2,3},{3,2},{4,5},{5,4},{6,7},{7,6},{8,9},{9,8},{10,11... | collective-permute-start | bytes 1572872 | tf_op jit(solution)/shard_map/ppermute | solution.py:24
  327.4 15.2 %collective-permute-start.16 = (bf16[512,512]{1,0:T(8,128)(2,1)}, bf16[512,512]{1,0:T(8,128)(2,1)S(1)}, u32[]{:S(2)}, u32[]{:S(2)}) collective-permute-start(bf16[512,512]{1,0:T(8,128)(2,1)} %get-tuple-element.226), channel_id=1, source_target_pairs={{0,2},{1,3},{2,0},{3,1},{4,6},{5,7},{6,4},{7,5},{8,10},{9,11},{10,... | collective-permute-start | bytes 1572872 | tf_op jit(solution)/shard_map/ppermute | solution.py:24
  329.7 24.8 %collective-permute-start.17 = (bf16[512,512]{1,0:T(8,128)(2,1)}, bf16[512,512]{1,0:T(8,128)(2,1)S(1)}, u32[]{:S(2)}, u32[]{:S(2)}) collective-permute-start(bf16[512,512]{1,0:T(8,128)(2,1)} %get-tuple-element.226), channel_id=1, source_target_pairs={{0,3},{1,2},{2,1},{3,0},{4,7},{5,6},{6,5},{7,4},{8,11},{9,10},{10,... | collective-permute-start | bytes 1572872 | tf_op jit(solution)/shard_map/ppermute | solution.py:24
  333.8 26.4 %collective-permute-start.24 = (s32[2,256]{1,0:T(2,128)S(1)}, s32[2,256]{1,0:T(2,128)S(1)}, u32[]{:S(2)}, u32[]{:S(2)}) collective-permute-start(s32[2,256]{1,0:T(2,128)S(1)} %collective-permute-done.22), channel_id=1, source_target_pairs={{0,4},{4,8},{8,12},{12,16},{16,20},{20,24},{24,28},{28,32},{32,36}... | collective-permute-start | bytes 6152 | tf_op jit(solution)/shard_map/ppermute | solution.py:19
  340.1 35.8 %collective-permute-start.28 = (bf16[256,2048]{0,1:T(8,128)(2,1)}, bf16[256,2048]{0,1:T(8,128)(2,1)}, u32[]{:S(2)}, u32[]{:S(2)}) collective-permute-start(bf16[256,2048]{0,1:T(8,128)(2,1)} %all-gather.11.cloned.1.call-done), channel_id=1, source_target_pairs={{0,128},{128,0},{1,129},{129,1},{2,130},{130,2},{3,131},{131,3},{4... | collective-permute-start | bytes 3145736 | tf_op jit(solution)/shard_map/ppermute | solution.py:24
  359.5 22.1 %collective-permute-start.19 = (bf16[2,256,2,2,64]{1,0,4,3,2:T(2,128)(2,1)S(1)}, bf16[2,256,2,2,64]{1,0,4,3,2:T(2,128)(2,1)}, u32[]{:S(2)}, u32[]{:S(2)}) collective-permute-start(bf16[2,256,2,2,64]{1,0,4,3,2:T(2,128)(2,1)S(1)} %slice.50), channel_id=1, source_target_pairs={{0,128},{128,0},{1,129},{129,1},{2,130},{130,2},{3,131},{131,3},{4... | collective-permute-start | bytes 786440 | tf_op jit(solution)/shard_map/ppermute | solution.py:24
  386.0 16.5 %collective-permute-start.21 = (bf16[2,256,2,2,64]{1,0,4,3,2:T(2,128)(2,1)}, bf16[2,256,2,2,64]{1,0,4,3,2:T(2,128)(2,1)S(1)}, u32[]{:S(2)}, u32[]{:S(2)}) collective-permute-start(bf16[2,256,2,2,64]{1,0,4,3,2:T(2,128)(2,1)} %collective-permute-done.19), channel_id=1, source_target_pairs={{0,4},{4,8},{8,12},{12,16},{16,20},{20,24},{24,28},{28,32},{32,36}... | collective-permute-start | bytes 786440 | tf_op jit(solution)/shard_map/ppermute | solution.py:19
  390.6 36.5 %collective-permute-start.29 = (bf16[512,512]{1,0:T(8,128)(2,1)}, bf16[512,512]{1,0:T(8,128)(2,1)}, u32[]{:S(2)}, u32[]{:S(2)}) collective-permute-start(bf16[512,512]{1,0:T(8,128)(2,1)} %get-tuple-element.218), channel_id=1, source_target_pairs={{0,1},{1,0},{2,3},{3,2},{4,5},{5,4},{6,7},{7,6},{8,9},{9,8},{10,11... | collective-permute-start | bytes 1572872 | tf_op jit(solution)/shard_map/ppermute | solution.py:24
  392.1 36.6 %collective-permute-start.30 = (bf16[512,512]{1,0:T(8,128)(2,1)}, bf16[512,512]{1,0:T(8,128)(2,1)}, u32[]{:S(2)}, u32[]{:S(2)}) collective-permute-start(bf16[512,512]{1,0:T(8,128)(2,1)} %get-tuple-element.217), channel_id=1, source_target_pairs={{0,2},{1,3},{2,0},{3,1},{4,6},{5,7},{6,4},{7,5},{8,10},{9,11},{10,... | collective-permute-start | bytes 1572872 | tf_op jit(solution)/shard_map/ppermute | solution.py:24
  393.8 34.9 %collective-permute-start.31 = (bf16[512,512]{1,0:T(8,128)(2,1)}, bf16[512,512]{1,0:T(8,128)(2,1)}, u32[]{:S(2)}, u32[]{:S(2)}) collective-permute-start(bf16[512,512]{1,0:T(8,128)(2,1)} %get-tuple-element.216), channel_id=1, source_target_pairs={{0,3},{1,2},{2,1},{3,0},{4,7},{5,6},{6,5},{7,4},{8,11},{9,10},{10,... | collective-permute-start | bytes 1572872 | tf_op jit(solution)/shard_map/ppermute | solution.py:24
  427.2 24.7 %collective-permute-start.27 = (bf16[512,512]{0,1:T(8,128)(2,1)S(1)}, bf16[512,512]{0,1:T(8,128)(2,1)S(1)}, u32[]{:S(2)}, u32[]{:S(2)}) collective-permute-start(bf16[512,512]{0,1:T(8,128)(2,1)S(1)} %bitcast.201), channel_id=1, source_target_pairs={{0,3},{1,2},{2,1},{3,0},{4,7},{5,6},{6,5},{7,4},{8,11},{9,10},{10,... | collective-permute-start | bytes 1572872 | tf_op jit(solution)/shard_map/ppermute | solution.py:24
  (17 other events, 322.6 us)
Sparse Core Ops, SparseCore 0:
  9.9 76.2 all-gather.4
  88.8 73.1 all-gather.6
  164.6 75.0 all-gather.8
  242.1 73.9 all-gather.10
